TPU v7x, 512 devices: a whole 4x4x16 slice. The times are simulated.
512 devices in a mesh: ctx: 64 (over z_lo, y, core), wa: 8 (over z_hi, x).
Axes of the slice: x: 4, y: 4, z: 16 (z_hi: 2, z_lo: 8; z = z_hi * 8 + z_lo), core: 2. Of those that a mesh axis runs over, the one named last changes fastest.
Arguments:
- q_nope: bfloat16 [512, 8192], P('ctx', 'wa'), may hold values from -6 to 6
- q_rope: bfloat16 [512, 4096], P('ctx', 'wa'), may hold values from -100 to 100
- w_uk: bfloat16 [64, 128, 512], P('wa'), may hold values from -0.25 to 0.25
- w_uv: bfloat16 [64, 512, 128], P('wa'), may hold values from -0.25 to 0.25
- cache: bfloat16 [32768, 576], P('ctx'), may hold values from -16 to 16
- cache_scale: float32 [32768], P('ctx'), may hold values from 0.5 to 2, as said below
- new_latent: bfloat16 [512, 576], P('ctx'), may hold values from -16 to 16
- cache_doc: int32 [512], P('ctx'), may hold values from 0 to 15
- new_lengths: int32 [16], replicated, may hold values from 1 to 128, 512 in all
Outputs:
- attn_out: bfloat16 [512, 8192], P('ctx', 'wa')
Inputs may be any that keep to these rules, and one draw needn't show every extreme that they name: `cache_scale`: each scale is 0.5, 1 or 2.
All inputs are finite; a program needn't handle non-finite values.
Results may differ from a plain program's by a relative error of at most 0.0064.
Values may be sent and summed in bfloat16 or wider, within the bound.
No kernel may reach another device: no remote copies, remote signals or barrier semaphores. Data moves between devices by JAX's collectives and lax.ppermute only.
A program may use at most 64 MiB of HBM per device.

v0:
```python
import jax
import jax.numpy as jnp
import numpy as np
from jax import lax
from jax.sharding import Mesh, PartitionSpec as P

CHIP_PARTS = ("cz", "cy")
CORE = "cc"


def doc_index(position, new_lengths):
    ends = jnp.cumsum(new_lengths)
    return jnp.sum((ends[None, :] <= position[:, None]).astype(jnp.int32), axis=1)


def absorb_rows(nope_rows, w_uk):
    row_count = nope_rows.shape[0]
    heads_dev, nope_dim, latent_dim = w_uk.shape
    shaped = nope_rows.reshape(row_count, heads_dev, nope_dim)
    absorbed = jnp.einsum("thn,hnl->thl", shaped, w_uk, preferred_element_type=jnp.float32)
    return absorbed.astype(jnp.bfloat16)


def chip_index():
    index = lax.axis_index(CHIP_PARTS[0])
    for name in CHIP_PARTS[1:]:
        index = index * lax.axis_size(name) + lax.axis_index(name)
    return index


def gather_rows(x):
    for name in reversed(CHIP_PARTS):
        x = lax.all_gather(x, name, axis=0, tiled=True)
    return x


def scatter_rows(x):
    for name in CHIP_PARTS:
        x = lax.psum_scatter(x, name, scatter_dimension=0, tiled=True)
    return x


def merge_stats(stats, heads_dev):
    for name in reversed(CHIP_PARTS):
        group = lax.all_gather(stats, name, axis=0, tiled=False)
        peak = jnp.max(group[:, :, :heads_dev], axis=0)
        shifted = jnp.where(jnp.isfinite(peak), peak, jnp.zeros_like(peak))
        scale = jnp.exp(group[:, :, :heads_dev] - shifted[None])
        total = jnp.sum(scale * group[:, :, heads_dev:], axis=0)
        stats = jnp.concatenate([peak, total], axis=1)
    return (stats[:, :heads_dev], stats[:, heads_dev:])


def swap_cores(x):
    return lax.ppermute(x, CORE, [(0, 1), (1, 0)])


def body(q_nope, q_rope, w_uk, w_uv, cache, cache_scale, new_latent, cache_doc, new_lengths):
    tok_rows = q_nope.shape[0]
    heads_dev, nope_dim, latent_dim = w_uk.shape
    value_dim = w_uv.shape[2]
    rope_dim = q_rope.shape[1] // heads_dev
    cores = lax.axis_size(CORE)
    chips = 1
    for name in CHIP_PARTS:
        chips = chips * lax.axis_size(name)
    q_rows = tok_rows * chips
    my_chip = chip_index()
    my_core = lax.axis_index(CORE)
    other_core = 1 - my_core
    score_scale = (nope_dim + rope_dim) ** (-0.5)
    dequant = (cache.astype(jnp.float32) * cache_scale[:, None]).astype(jnp.bfloat16)
    own_keys = jnp.concatenate([dequant, new_latent], axis=0)
    other_keys = swap_cores(own_keys)
    other_doc = swap_cores(cache_doc)
    own_q = jnp.concatenate([q_nope, q_rope], axis=1)
    all_q = gather_rows(own_q)
    nope_width = heads_dev * nope_dim
    all_lat = absorb_rows(all_q[:, :nope_width], w_uk)
    all_rope = all_q[:, nope_width:]
    query = jnp.concatenate([all_lat, all_rope.reshape(q_rows, heads_dev, rope_dim)], axis=2)
    cache_len = cache.shape[0]
    block_len = cache_len // cache_doc.shape[0]
    row = jnp.arange(q_rows, dtype=jnp.int32)
    query_pos = (row // tok_rows * cores + my_core) * tok_rows + row % tok_rows
    query_doc = doc_index(query_pos, new_lengths)

    def key_meta(core, docs):
        new_pos = (my_chip * cores + core) * tok_rows + jnp.arange(tok_rows, dtype=jnp.int32)
        key_doc = jnp.concatenate([jnp.repeat(docs, block_len), doc_index(new_pos, new_lengths)])
        key_pos = jnp.concatenate([jnp.full((cache_len,), -1, dtype=jnp.int32), new_pos])
        return (key_doc, key_pos)

    own_doc, own_pos = key_meta(my_core, cache_doc)
    far_doc, far_pos = key_meta(other_core, other_doc)
    key_rows = jnp.concatenate([own_keys, other_keys], axis=0)
    key_doc = jnp.concatenate([own_doc, far_doc])
    key_pos = jnp.concatenate([own_pos, far_pos])
    allowed = (query_doc[:, None] == key_doc[None, :]) & (key_pos[None, :] <= query_pos[:, None])
    score = (
        jnp.einsum("qhl,kl->qhk", query, key_rows, preferred_element_type=jnp.float32) * score_scale
    )
    masked = jnp.where(allowed[:, None, :], score, -jnp.inf)
    local_max = jnp.max(masked, axis=2)
    shift = jnp.where(jnp.isfinite(local_max), local_max, jnp.zeros_like(local_max))
    weight = jnp.exp(masked - shift[:, :, None])
    totals = jnp.sum(weight, axis=2)
    weight_low = weight.astype(jnp.bfloat16)
    part_lat = jnp.einsum(
        "qhk,kl->qhl", weight_low, key_rows[:, :latent_dim], preferred_element_type=jnp.float32
    ).astype(jnp.bfloat16)
    numerator = jnp.einsum("qhl,hlv->qhv", part_lat, w_uv, preferred_element_type=jnp.float32)
    row_max, row_total = merge_stats(jnp.concatenate([local_max, totals], axis=1), heads_dev)
    factor = jnp.exp(local_max - row_max)
    scaled = (numerator * factor[:, :, None]).reshape(q_rows, heads_dev * value_dim)
    own_numer = scatter_rows(scaled).reshape(tok_rows, heads_dev, value_dim)
    own_total = lax.dynamic_slice_in_dim(row_total, my_chip * tok_rows, tok_rows, axis=0)
    result = own_numer / own_total[:, :, None]
    return result.astype(jnp.bfloat16).reshape(tok_rows, heads_dev * value_dim)


def solution(mesh):
    ctx_shape = (8, 4, 2)
    grid = np.asarray(mesh.devices).reshape(ctx_shape + (mesh.shape["wa"],))
    fine = Mesh(grid, CHIP_PARTS + (CORE, "wa"))
    rows = CHIP_PARTS + (CORE,)
    placed = (
        P(rows, "wa"),
        P(rows, "wa"),
        P("wa", None, None),
        P("wa", None, None),
        P(rows, None),
        P(rows),
        P(rows, None),
        P(rows),
        P(),
    )
    return jax.shard_map(body, mesh=fine, in_specs=placed, out_specs=P(rows, "wa"), check_vma=False)
```

profile of v0, /device:TPU:2, one launch (start us, length us, event | category | flops | bytes accessed | tf_op | source)
XLA Modules:
  0.0 268.3 jit_solution(17568479425091766491)
XLA Ops:
  6.5 0.0 copy-start
  6.5 0.0 copy-start.7
  6.5 0.0 copy-start.6
  6.5 0.0 copy-start.5
  6.5 0.0 reduce-scatter.3.cloned.1.call-start
  6.6 2.1 collective-permute-start
  8.6 0.9 copy.64
  9.5 0.0 copy-start.2
  9.5 1.2 multiply_convert_fusion
  10.8 0.1 pad_maximum_fusion
  10.8 1.1 copy.63
  12.0 2.4 collective-permute-start.1
  14.4 0.0 copy-done.7
  14.4 0.1 copy.57
  14.5 0.1 reduce
  14.7 0.0 copy-done.6
  14.7 0.0 copy-done.5
  14.7 0.0 copy-done.2
  14.7 12.4 %all_gather.18 = bf16[32,1536]{1,0:T(8,128)(2,1)S(1)} all-gather(bf16[8,1536]{1,0:T(8,128)(2,1)S(1)} %pad_maximum_fusion.1), channel_id=1, replica_groups=mesh['cz'=8,'cy'=4,'cc'=2,'wa'=8] {'cy'}, dimensions={0}, use_global_device_ids=true | all-gather | bytes 122880 | tf_op jit(solution)/shard_map/all_gather | solution.py:33
  27.2 51.2 %all_gather.19 = bf16[256,1536]{1,0:T(8,128)(2,1)S(1)} all-gather(bf16[32,1536]{1,0:T(8,128)(2,1)S(1)} %all_gather.18), channel_id=1, replica_groups=mesh['cz'=8,'cy'=4,'cc'=2,'wa'=8] {'cz'}, dimensions={0}, use_global_device_ids=true | all-gather | bytes 884736 | tf_op jit(solution)/shard_map/all_gather | solution.py:33
  78.4 0.1 slice.30
  78.4 0.0 copy-start.8
  78.4 0.2 copy.75
  78.6 0.1 convert_reduce_fusion
  78.7 0.0 copy-done
  78.7 2.1 convert_bitcast_fusion
  80.8 0.0 copy-start.3
  80.9 0.0 copy-done.8
  80.9 0.1 broadcast_in_dim.12
  80.9 0.1 reshape.143
  81.0 0.1 copy.76
  81.2 0.3 copy.61
  81.5 0.1 concatenate.26
  81.6 0.2 convert_reduce_fusion.1
  81.8 0.0 collective-permute-done
  81.8 0.1 broadcast_in_dim.13
  81.9 0.1 reshape.144
  81.9 0.1 concatenate.25
  82.0 0.7 compare_and_fusion
  82.8 0.0 collective-permute-done.1
  82.8 1.4 copy.65
  84.2 0.0 copy-done.3
  84.2 2.1 concatenate.30
  86.3 6.2 %fusion = (f32[256,8]{0,1:T(8,128)S(1)}, f32[256,8,1040]{0,2,1:T(8,128)S(1)}) fusion(pred[256,1040]{0,1:T(8,128)(4,1)S(1)} %compare_and_fusion, bf16[1040,576]{0,1:T(8,128)(2,1)} %concatenate.30, bf16[256,8,64]{2,0,1:T(8,128)(2,1)S(1)} %copy.61, bf16[256,8,512]{2,0,1:T(8,128)(2,1)} %convert_bitcast_fusion), kind=kOutput, calls=%fused_computation.2 | convolution fusion | flops 2464774144 | bytes 12351488 | tf_op jit(solution)/shard_map/qhl,kl->qhk/dot_general | solution.py:101
  92.5 0.0 copy-start.1
  92.5 0.0 copy-start.4
  92.5 1.7 fusion.1
  94.3 1.5 copy-done.1
  95.8 11.9 %all-gather = f32[1024,16]{0,1:T(8,128)S(1)} all-gather(f32[256,16]{0,1:T(8,128)S(1)} %pad_maximum_fusion.2), channel_id=2, replica_groups=mesh['cz'=8,'cy'=4,'cc'=2,'wa'=8] {'cy'}, dimensions={0}, use_global_device_ids=true | all-gather | bytes 81920 | tf_op jit(solution)/shard_map/all_gather | solution.py:45
  107.8 46.6 %all-gather.1 = f32[2048,16]{0,1:T(8,128)S(1)} all-gather(f32[256,16]{0,1:T(8,128)S(1)} %pad_maximum_fusion.3), channel_id=3, replica_groups=mesh['cz'=8,'cy'=4,'cc'=2,'wa'=8] {'cz'}, dimensions={0}, use_global_device_ids=true | all-gather | bytes 147456 | tf_op jit(solution)/shard_map/all_gather | solution.py:45
  154.5 0.0 copy-done.4
  154.5 8.4 %fusion.24 = f32[256,8,128]{0,2,1:T(8,128)} fusion(bf16[8,512,128]{2,1,0:T(8,128)(2,1)} %param.12, f32[256,8,1040]{0,2,1:T(8,128)} %copy-done.1, f32[256,8]{0,1:T(8,128)S(1)} %is-finite_select_fusion.2, pred[256,1040]{0,1:T(8,128)(4,1)S(1)} %compare_and_fusion, bf16[1040,576]{0,1:T(8,128)(2,1)S(1)} %copy-done.4, f32[256,8]{0,1:T(8,128)S(1)} %get-tuple-element.8), kind=kOutput, calls=%fused_computation.18 | convolution fusion | flops 2459303936 | bytes 12079104 | tf_op jit(solution)/shard_map/qhl,hlv->qhv/dot_general | solution.py:112
  162.9 2.5 copy.69
  165.4 0.0 reduce-scatter.3.cloned.1.call-update
  165.5 0.0 reduce-scatter.5.cloned.1.call-start
  165.5 70.0 %reduce-scatter.3.cloned.1.call-done = f32[32,1024]{1,0:T(8,128)} async-done(((f32[256,1024]{1,0:T(8,128)}), f32[32,1024]{1,0:T(8,128)}) %reduce-scatter.3.cloned.1.call-update) | async-done | bytes 131088 | tf_op jit(solution)/shard_map/reduce_scatter | solution.py:39
  235.5 0.0 reduce-scatter.5.cloned.1.call-update
  235.6 0.1 constant_dynamic-slice_fusion
  235.7 24.4 %reduce-scatter.5.cloned.1.call-done = f32[8,1024]{1,0:T(8,128)} async-done(((f32[32,1024]{1,0:T(8,128)}), f32[8,1024]{1,0:T(8,128)}) %reduce-scatter.5.cloned.1.call-update) | async-done | bytes 32784 | tf_op jit(solution)/shard_map/reduce_scatter | solution.py:39
  260.1 1.4 fusion.32
  (17 shorter events, 0.3 us)
Async XLA Ops:
  6.5 72.2 %copy-start = (bf16[8,128,512]{2,1,0:T(8,128)(2,1)S(1)}, bf16[8,128,512]{2,1,0:T(8,128)(2,1)}, u32[]{:S(2)}) copy-start(bf16[8,128,512]{2,1,0:T(8,128)(2,1)} %param.11) | copy-start | bytes 3145732
  6.5 7.9 %copy-start.7 = (s32[16]{0:T(128)S(1)}, s32[16]{0:T(128)}, u32[]{:S(2)}) copy-start(s32[16]{0:T(128)} %param.17) | copy-start | bytes 196
  6.5 8.1 %copy-start.6 = (bf16[8,512]{1,0:T(8,128)(2,1)S(1)}, bf16[8,512]{1,0:T(8,128)(2,1)}, u32[]{:S(2)}) copy-start(bf16[8,512]{1,0:T(8,128)(2,1)} %param.10) | copy-start | bytes 24580
  6.5 8.1 %copy-start.5 = (bf16[8,1024]{1,0:T(8,128)(2,1)S(1)}, bf16[8,1024]{1,0:T(8,128)(2,1)}, u32[]{:S(2)}) copy-start(bf16[8,1024]{1,0:T(8,128)(2,1)} %param.9) | copy-start | bytes 49156
  6.5 229.0 %reduce-scatter.3.cloned.1.call-start = ((), (), s32[]{:S(2)}) async-start(), calls=%async_computation.2 | async-start | bytes 1179648 | tf_op jit(solution)/shard_map/reduce_scatter | solution.py:39
  6.6 75.2 %collective-permute-start = (s32[8]{0:T(128)}, s32[8]{0:T(128)S(1)}, u32[]{:S(2)}, u32[]{:S(2)}) collective-permute-start(s32[8]{0:T(128)} %param.16), channel_id=1, source_target_pairs={{0,8},{8,0},{1,9},{9,1},{2,10},{10,2},{3,11},{11,3},{4,12},{12,4},... | collective-permute-start | bytes 104 | tf_op jit(solution)/shard_map/ppermute | solution.py:55
  9.5 5.2 %copy-start.2 = (bf16[8,576]{0,1:T(8,128)(2,1)}, bf16[8,576]{0,1:T(8,128)(2,1)S(1)}, u32[]{:S(2)}) copy-start(bf16[8,576]{0,1:T(8,128)(2,1)S(1)} %copy.64) | copy-start | bytes 27652
  12.0 70.8 %collective-permute-start.1 = (bf16[520,576]{1,0:T(8,128)(2,1)}, bf16[520,576]{1,0:T(8,128)(2,1)}, u32[]{:S(2)}, u32[]{:S(2)}) collective-permute-start(bf16[520,576]{1,0:T(8,128)(2,1)} %copy.63), channel_id=1, source_target_pairs={{0,8},{8,0},{1,9},{9,1},{2,10},{10,2},{3,11},{11,3},{4,12},{12,4},... | collective-permute-start | bytes 1797128 | tf_op jit(solution)/shard_map/ppermute | solution.py:55
  78.4 2.4 copy-start.8
  80.8 3.4 %copy-start.3 = (bf16[8,576]{0,1:T(8,128)(2,1)S(1)}, bf16[8,576]{0,1:T(8,128)(2,1)}, u32[]{:S(2)}) copy-start(bf16[8,576]{0,1:T(8,128)(2,1)} %copy-done.2) | copy-start | bytes 27652
  92.5 3.3 %copy-start.1 = (f32[256,8,1040]{0,2,1:T(8,128)}, f32[256,8,1040]{0,2,1:T(8,128)S(1)}, u32[]{:S(2)}) copy-start(f32[256,8,1040]{0,2,1:T(8,128)S(1)} %get-tuple-element.10) | copy-start | bytes 25559044
  92.5 62.0 %copy-start.4 = (bf16[1040,576]{0,1:T(8,128)(2,1)S(1)}, bf16[1040,576]{0,1:T(8,128)(2,1)}, u32[]{:S(2)}) copy-start(bf16[1040,576]{0,1:T(8,128)(2,1)} %concatenate.30) | copy-start | bytes 3594244
  165.5 94.6 %reduce-scatter.5.cloned.1.call-start = ((), (), s32[]{:S(2)}) async-start(), calls=%async_computation.3 | async-start | bytes 163840 | tf_op jit(solution)/shard_map/reduce_scatter | solution.py:39
Sparse Core Ops, SparseCore 0:
  165.6 69.9 reduce-scatter.2
  238.3 21.6 reduce-scatter.4
where the time goes:
time: 269 us; the launch traced here: 268 us
  blocking collectives  122 us (45%)
  waiting for transfers between devices  94.4 us (35%)
  matrix products  16.7 us (6%)
  between operations  13.7 us (5%)
  local copies, waits for them, and re-layouts  11.1 us (4%)
  other arithmetic  5.83 us (2%)
  starting transfers between devices  4.52 us (2%)
    reduce_scatter x2, waiting for transfers between devices, scatter_rows(): x = lax.psum_scatter(x, name, scatter_dimension=0, tiled=True)  94.4 us
    all_gather x2, blocking collectives, gather_rows(): x = lax.all_gather(x, name, axis=0, tiled=True)  63.7 us
    all_gather x2, blocking collectives, merge_stats(): group = lax.all_gather(stats, name, axis=0, tiled=False)  58.4 us
    dot_general x1, matrix products, body(): jnp.einsum('qhl,hlv->qhv', part_lat, w_uv, preferred_element_type=jnp.flo...  8.42 us
    dot_general x1, matrix products, body(): jnp.einsum('qhl,kl->qhk', query, key_rows, preferred_element_type=jnp.flo...  6.18 us
  transfers between devices with their start and end apart: 4, of which 2 were waited for; matrix products, arithmetic and copies ran while one was open for 3% of the time, Pallas kernels for 0%

commit v1 on v0

--- a/solution.py
+++ b/solution.py
@@ -30,7 +30,9 @@
 
 def gather_rows(x):
     for name in reversed(CHIP_PARTS):
-        x = lax.all_gather(x, name, axis=0, tiled=True)
+        x = jnp.concatenate(
+            lax.all_to_all(jnp.stack([x] * lax.axis_size(name)), name, 0, 0), axis=0
+        )
     return x
 
 

time: 269 us -> 248 us (0.922)
  blocking collectives: 122 us -> 68.4 us
  waiting for transfers between devices: 94.4 us -> 115 us
  starting transfers between devices: 4.52 us -> 17.1 us
  matrix products: 16.7 us -> 13.4 us
  local copies, waits for them, and re-layouts: 11.1 us -> 14.1 us
    all_gather x2 -> x0, blocking collectives: 63.7 us -> none  [gather_rows(): x = lax.all_gather(x, name, axis=0, tiled=True)]
    all_to_all x0 -> x1, waiting for transfers between devices: none -> 26.8 us  [gather_rows(): lax.all_to_all(jnp.stack([x] * lax.axis_size(name)), name, 0, 0)]
    all_to_all x0 -> x1, starting transfers between devices: none -> 12.7 us  [gather_rows(): lax.all_to_all(jnp.stack([x] * lax.axis_size(name)), name, 0, 0)]
    all_to_all x0 -> x1, blocking collectives: none -> 10.1 us  [gather_rows(): lax.all_to_all(jnp.stack([x] * lax.axis_size(name)), name, 0, 0)]
    reduce_scatter x2, waiting for transfers between devices: 94.4 us -> 88.2 us  [scatter_rows(): x = lax.psum_scatter(x, name, scatter_dimension=0, tiled=True)]
  transfers between devices with their start and end apart: 4 -> 5, of which waited for: 2 -> 3; matrix products, arithmetic and copies ran while one was open for 3% -> 3% of each run, Pallas kernels for 0% -> 0%
where the time goes in v1:
time: 248 us
  waiting for transfers between devices  115 us (46%)
  blocking collectives  68.4 us (28%)
  starting transfers between devices  17.1 us (7%)
  local copies, waits for them, and re-layouts  14.1 us (6%)
  between operations  13.7 us (6%)
  matrix products  13.4 us (5%)
  other arithmetic  6.2 us (2%)
    reduce_scatter x2, waiting for transfers between devices, scatter_rows(): x = lax.psum_scatter(x, name, scatter_dimension=0, tiled=True)  88.2 us
    all_gather x2, blocking collectives, merge_stats(): group = lax.all_gather(stats, name, axis=0, tiled=False)  58.3 us
    all_to_all x1, waiting for transfers between devices, gather_rows(): lax.all_to_all(jnp.stack([x] * lax.axis_size(name)), name, 0, 0)  26.8 us
    all_to_all x1, starting transfers between devices, gather_rows(): lax.all_to_all(jnp.stack([x] * lax.axis_size(name)), name, 0, 0)  12.7 us
    all_to_all x1, blocking collectives, gather_rows(): lax.all_to_all(jnp.stack([x] * lax.axis_size(name)), name, 0, 0)  10.1 us
    dot_general x1, matrix products, body(): jnp.einsum('qhl,hlv->qhv', part_lat, w_uv, preferred_element_type=jnp.flo...  8.41 us
  transfers between devices with their start and end apart: 5, of which 3 were waited for; matrix products, arithmetic and copies ran while one was open for 3% of the time, Pallas kernels for 0%

profile of v1, /device:TPU:2, one launch (start us, length us, event | category | flops | bytes accessed | tf_op | source)
XLA Modules:
  0.0 247.8 jit_solution(4422051015866214142)
XLA Ops:
  6.5 0.0 copy-start
  6.5 0.0 copy-start.9
  6.5 0.0 copy-start.6
  6.5 0.0 copy-start.7
  6.5 0.0 copy-start.4
  6.5 0.9 pad_maximum_fusion.1
  7.4 10.1 %all_to_all.10 = bf16[4,8,1536]{2,1,0:T(8,128)(2,1)S(1)} all-to-all(bf16[4,8,1536]{2,1,0:T(8,128)(2,1)S(1)} %stack.4), channel_id=1, replica_groups=mesh['cz'=8,'cy'=4,'cc'=2,'wa'=8] {'cy'}, dimensions={0} | all-to-all | bytes 196608 | tf_op jit(solution)/shard_map/all_to_all | solution.py:34
  17.5 1.0 stack.5
  18.5 12.7 %all-to-all-start.1 = ((bf16[8,32,1536]{2,1,0:T(8,128)(2,1)}), bf16[8,32,1536]{2,1,0:T(8,128)(2,1)S(1)}, u32[]{:S(2)}, u32[]{:S(2)}) async-start(bf16[8,32,1536]{2,1,0:T(8,128)(2,1)} %stack.5), calls=%async_computation.1 | async-start | bytes 1572864 | tf_op jit(solution)/shard_map/all_to_all | solution.py:34
  31.1 0.0 reduce-scatter.3.cloned.1.call-start
  31.2 0.0 copy-done.9
  31.2 1.9 collective-permute-start
  33.1 0.0 copy-done.6
  33.1 0.2 copy.51
  33.3 0.0 copy-done.7
  33.3 0.0 copy-done.4
  33.3 0.1 multiply_convert_fusion
  33.4 0.1 pad_maximum_fusion
  33.5 1.1 copy.50
  34.6 2.4 collective-permute-start.1
  37.1 0.0 copy-done.8
  37.1 0.1 copy.44
  37.2 0.1 reduce
  37.3 0.1 convert_reduce_fusion
  37.4 0.1 broadcast_in_dim.12
  37.5 0.1 reshape.150
  37.6 0.1 concatenate.26
  37.6 0.2 convert_reduce_fusion.1
  37.9 0.0 collective-permute-done
  37.9 0.1 broadcast_in_dim.13
  37.9 0.1 reshape.151
  38.0 0.1 concatenate.25
  38.1 1.4 compare_and_fusion
  39.5 0.0 collective-permute-done.1
  39.5 1.4 copy.52
  40.9 2.0 concatenate.30
  43.0 26.8 %all-to-all-done.1 = bf16[8,32,1536]{2,1,0:T(8,128)(2,1)S(1)} async-done(((bf16[8,32,1536]{2,1,0:T(8,128)(2,1)}), bf16[8,32,1536]{2,1,0:T(8,128)(2,1)S(1)}, u32[]{:S(2)}, u32[]{:S(2)}) %all-to-all-start.1) | async-done | bytes 786464 | tf_op jit(solution)/shard_map/all_to_all | solution.py:34
  69.7 0.7 slice.31
  70.5 0.1 slice.30
  70.5 0.2 copy.45
  70.7 0.0 copy-start.2
  70.7 0.0 copy-start.3
  70.8 1.2 copy.47
  72.0 1.0 copy.48
  73.0 0.0 copy-done
  73.0 0.8 convert_bitcast_fusion
  73.8 0.0 copy-done.2
  73.8 0.0 copy-done.3
  73.8 0.3 copy-done.5
  74.0 4.3 %fusion = (f32[256,8]{0,1:T(8,128)S(1)}, f32[256,8,1040]{0,2,1:T(8,128)S(1)}) fusion(pred[256,1040]{0,1:T(8,128)(4,1)S(1)} %copy-done.3, bf16[1040,576]{0,1:T(8,128)(2,1)S(1)} %copy-done.2, bf16[256,8,64]{2,0,1:T(8,128)(2,1)S(1)} %copy-done.5, bf16[256,8,512]{2,0,1:T(8,128)(2,1)S(1)} %convert_bitcast_fusion), kind=kOutput, calls=%fused_computation.2 | convolution fusion | flops 2464774144 | bytes 12351488 | tf_op jit(solution)/shard_map/qhl,kl->qhk/dot_general | solution.py:103
  78.3 0.0 copy-start.1
  78.3 1.7 fusion.1
  80.1 1.5 copy-done.1
  81.6 11.9 %all-gather = f32[1024,16]{0,1:T(8,128)S(1)} all-gather(f32[256,16]{0,1:T(8,128)S(1)} %pad_maximum_fusion.2), channel_id=2, replica_groups=mesh['cz'=8,'cy'=4,'cc'=2,'wa'=8] {'cy'}, dimensions={0}, use_global_device_ids=true | all-gather | bytes 81920 | tf_op jit(solution)/shard_map/all_gather | solution.py:47
  93.6 46.5 %all-gather.1 = f32[2048,16]{0,1:T(8,128)S(1)} all-gather(f32[256,16]{0,1:T(8,128)S(1)} %pad_maximum_fusion.3), channel_id=3, replica_groups=mesh['cz'=8,'cy'=4,'cc'=2,'wa'=8] {'cz'}, dimensions={0}, use_global_device_ids=true | all-gather | bytes 147456 | tf_op jit(solution)/shard_map/all_gather | solution.py:47
  140.1 8.4 %fusion.24 = f32[256,8,128]{0,2,1:T(8,128)} fusion(bf16[8,512,128]{2,1,0:T(8,128)(2,1)} %param.12, f32[256,8,1040]{0,2,1:T(8,128)} %copy-done.1, f32[256,8]{0,1:T(8,128)S(1)} %is-finite_select_fusion.2, pred[256,1040]{0,1:T(8,128)(4,1)S(1)} %copy-done.3, bf16[1040,576]{0,1:T(8,128)(2,1)S(1)} %copy-done.2, f32[256,8]{0,1:T(8,128)S(1)} %get-tuple-element.8), kind=kOutput, calls=%fused_computation.18 | convolution fusion | flops 2459303936 | bytes 12079104 | tf_op jit(solution)/shard_map/qhl,hlv->qhv/dot_general | solution.py:114
  148.5 2.5 %copy.56 = f32[256,1024]{1,0:T(8,128)} copy(f32[256,1024]{0,1:T(8,128)} %bitcast.38) | data formatting | bytes 2097152 | tf_op jit(solution)/shard_map/reshape | solution.py:117
  151.1 0.0 reduce-scatter.3.cloned.1.call-update
  151.1 0.0 reduce-scatter.5.cloned.1.call-start
  151.1 63.6 %reduce-scatter.3.cloned.1.call-done = f32[32,1024]{1,0:T(8,128)} async-done(((f32[256,1024]{1,0:T(8,128)}), f32[32,1024]{1,0:T(8,128)}) %reduce-scatter.3.cloned.1.call-update) | async-done | bytes 131088 | tf_op jit(solution)/shard_map/reduce_scatter | solution.py:41
  214.8 0.0 reduce-scatter.5.cloned.1.call-update
  214.8 0.1 constant_dynamic-slice_fusion
  214.9 24.6 %reduce-scatter.5.cloned.1.call-done = f32[8,1024]{1,0:T(8,128)} async-done(((f32[32,1024]{1,0:T(8,128)}), f32[8,1024]{1,0:T(8,128)}) %reduce-scatter.5.cloned.1.call-update) | async-done | bytes 32784 | tf_op jit(solution)/shard_map/reduce_scatter | solution.py:41
  239.5 1.4 fusion.32
  (18 shorter events, 0.3 us)
Async XLA Ops:
  6.5 66.5 %copy-start = (bf16[8,128,512]{2,1,0:T(8,128)(2,1)S(1)}, bf16[8,128,512]{2,1,0:T(8,128)(2,1)}, u32[]{:S(2)}) copy-start(bf16[8,128,512]{2,1,0:T(8,128)(2,1)} %param.11) | copy-start | bytes 3145732
  6.5 24.7 %copy-start.9 = (s32[8]{0:T(128)S(1)}, s32[8]{0:T(128)}, u32[]{:S(2)}) copy-start(s32[8]{0:T(128)} %param.16) | copy-start | bytes 100
  6.5 26.6 %copy-start.6 = (bf16[8,576]{1,0:T(8,128)(2,1)S(1)}, bf16[8,576]{1,0:T(8,128)(2,1)}, u32[]{:S(2)}) copy-start(bf16[8,576]{1,0:T(8,128)(2,1)} %param.15) | copy-start | bytes 27652
  6.5 26.8 %copy-start.7 = (f32[512]{0:T(512)S(1)}, f32[512]{0:T(512)}, u32[]{:S(2)}) copy-start(f32[512]{0:T(512)} %param.14) | copy-start | bytes 6148
  6.5 26.8 %copy-start.4 = (bf16[512,576]{0,1:T(8,128)(2,1)S(1)}, bf16[512,576]{0,1:T(8,128)(2,1)}, u32[]{:S(2)}) copy-start(bf16[512,576]{0,1:T(8,128)(2,1)} %param.13) | copy-start | bytes 1769476
  18.5 18.6 %copy-start.8 = (s32[16]{0:T(128)S(1)}, s32[16]{0:T(128)}, u32[]{:S(2)}) copy-start(s32[16]{0:T(128)} %param.17) | copy-start | bytes 196
  18.5 51.2 %all-to-all-start.1 = ((bf16[8,32,1536]{2,1,0:T(8,128)(2,1)}), bf16[8,32,1536]{2,1,0:T(8,128)(2,1)S(1)}, u32[]{:S(2)}, u32[]{:S(2)}) async-start(bf16[8,32,1536]{2,1,0:T(8,128)(2,1)} %stack.5), calls=%async_computation.1 | async-start | bytes 1572864 | tf_op jit(solution)/shard_map/all_to_all | solution.py:34
  31.1 183.6 %reduce-scatter.3.cloned.1.call-start = ((), (), s32[]{:S(2)}) async-start(), calls=%async_computation.4 | async-start | bytes 1179648 | tf_op jit(solution)/shard_map/reduce_scatter | solution.py:41
  31.2 6.7 %collective-permute-start = (s32[8]{0:T(128)S(1)}, s32[8]{0:T(128)S(1)}, u32[]{:S(2)}, u32[]{:S(2)}) collective-permute-start(s32[8]{0:T(128)S(1)} %copy-done.9), channel_id=1, source_target_pairs={{0,8},{8,0},{1,9},{9,1},{2,10},{10,2},{3,11},{11,3},{4,12},{12,4},... | collective-permute-start | bytes 104 | tf_op jit(solution)/shard_map/ppermute | solution.py:57
  34.6 4.8 %collective-permute-start.1 = (bf16[520,576]{1,0:T(8,128)(2,1)}, bf16[520,576]{1,0:T(8,128)(2,1)}, u32[]{:S(2)}, u32[]{:S(2)}) collective-permute-start(bf16[520,576]{1,0:T(8,128)(2,1)} %copy.50), channel_id=1, source_target_pairs={{0,8},{8,0},{1,9},{9,1},{2,10},{10,2},{3,11},{11,3},{4,12},{12,4},... | collective-permute-start | bytes 1797128 | tf_op jit(solution)/shard_map/ppermute | solution.py:57
  70.7 3.0 %copy-start.2 = (bf16[1040,576]{0,1:T(8,128)(2,1)S(1)}, bf16[1040,576]{0,1:T(8,128)(2,1)}, u32[]{:S(2)}) copy-start(bf16[1040,576]{0,1:T(8,128)(2,1)} %concatenate.30) | copy-start | bytes 3594244
  70.7 3.0 %copy-start.3 = (pred[256,1040]{0,1:T(8,128)(4,1)S(1)}, pred[256,1040]{0,1:T(8,128)(4,1)}, u32[]{:S(2)}) copy-start(pred[256,1040]{0,1:T(8,128)(4,1)} %compare_and_fusion) | copy-start | bytes 798724
  73.0 1.0 copy-start.5
  78.3 3.3 %copy-start.1 = (f32[256,8,1040]{0,2,1:T(8,128)}, f32[256,8,1040]{0,2,1:T(8,128)S(1)}, u32[]{:S(2)}) copy-start(f32[256,8,1040]{0,2,1:T(8,128)S(1)} %get-tuple-element.10) | copy-start | bytes 25559044
  151.1 88.4 %reduce-scatter.5.cloned.1.call-start = ((), (), s32[]{:S(2)}) async-start(), calls=%async_computation.5 | async-start | bytes 163840 | tf_op jit(solution)/shard_map/reduce_scatter | solution.py:41
Sparse Core Ops, SparseCore 0:
  151.2 63.4 reduce-scatter.2
  217.5 21.8 reduce-scatter.4
